TPU v7x, 512 devices: a whole 4x8x8 slice. The times are simulated.
512 devices in a mesh: dp: 16 (over y, core), tensor: 32 (over z, x).
Axes of the slice: x: 4, y: 8, z: 8, core: 2. Of those that a mesh axis runs over, the one named last changes fastest.
Arguments:
- layer_input: bfloat16 [65536, 8192], P('dp', 'tensor'), may hold values from -6 to 6
- output_grad: bfloat16 [65536, 1024], P(('dp', 'tensor')), may hold values from -6 to 6
- key_weight: bfloat16 [8192, 1024], P('tensor'), may hold values from -0.0625 to 0.0625
- adapter_down: bfloat16 [128, 16, 8192], P('dp', None, 'tensor'), may hold values from -0.0625 to 0.0625
- adapter_up: bfloat16 [128, 16, 1024], P('dp', None, 'tensor'), may hold values from -0.1875 to 0.1875
- segment_adapter: int32 [512], replicated, may hold values from 0 to 127
- adapter_slot: int32 [128], replicated, may hold values from 0 to 127, each once
- live_segments: int32 [16], P('dp'), may hold values from 1 to 32, as said below
Outputs:
- input_grad: bfloat16 [65536, 8192], P('dp', 'tensor')
- down_grad: bfloat16 [128, 16, 8192], P('dp', None, 'tensor')
- up_grad: bfloat16 [128, 16, 1024], P('dp', None, 'tensor')
Inputs may be any that keep to these rules, and one draw needn't show every extreme that they name: `live_segments`: some data group has all 32 segments live; a group's segments at or past its count are padding.
All inputs are finite; a program needn't handle non-finite values.
Results may differ from a plain program's by a relative error of at most 0.0057.
Values may be sent and summed in bfloat16 or wider, within the bound.
No kernel may reach another device: no remote copies, remote signals or barrier semaphores. Data moves between devices by JAX's collectives and lax.ppermute only.
A program may use at most 64 MiB of HBM per device.

v0:
```python
import jax
import jax.numpy as jnp
from jax import lax
from jax.sharding import PartitionSpec as P


def on_device(
    layer_input,
    output_grad,
    key_weight,
    adapter_down,
    adapter_up,
    segment_adapter,
    adapter_slot,
    live_segments,
):
    tensor_size = lax.axis_size("tensor")
    position = lax.axis_index("tensor")
    group_count = lax.axis_size("dp")
    group_index = lax.axis_index("dp")
    row_count = output_grad.shape[0]
    tok_group = layer_input.shape[0]
    width_shard = layer_input.shape[1]
    key_width = output_grad.shape[1]
    key_shard = key_width // tensor_size
    adapters = adapter_slot.shape[0]
    rank_dim = adapter_down.shape[1]
    seg_total = segment_adapter.shape[0]
    seg_group = seg_total // group_count
    seg_len = tok_group // seg_group
    per_owner = adapters // group_count
    slot_ids = jnp.arange(adapters, dtype=jnp.int32)
    lookup = segment_adapter[:, None] == slot_ids[None, :]
    every_slot = jnp.sum(jnp.where(lookup, adapter_slot[None, :], 0), axis=1)
    seg_slot = lax.dynamic_slice_in_dim(every_slot, group_index * seg_group, seg_group)
    local_rows = position * row_count + jnp.arange(row_count, dtype=jnp.int32)
    live_rows = local_rows // seg_len < live_segments[0]
    masked = jnp.where(live_rows[:, None], output_grad, jnp.zeros_like(output_grad))
    whole = lax.all_gather(masked, "tensor", axis=0, tiled=True)
    stores = (
        lax.all_gather(adapter_down, "dp", axis=0, tiled=True),
        lax.all_gather(adapter_up, "dp", axis=0, tiled=True),
    )
    choose = (seg_slot[:, None] == slot_ids[None, :]).astype(jnp.bfloat16)
    down_seg = jnp.dot(choose, stores[0].reshape(adapters, -1), preferred_element_type=jnp.float32)
    down_seg = down_seg.astype(jnp.bfloat16).reshape(seg_group, rank_dim, width_shard)
    up_seg = jnp.dot(choose, stores[1].reshape(adapters, -1), preferred_element_type=jnp.float32)
    up_seg = up_seg.astype(jnp.bfloat16).reshape(seg_group, rank_dim, key_shard)
    own_keys = lax.dynamic_slice_in_dim(whole, position * key_shard, key_shard, 1).reshape(
        seg_group, seg_len, key_shard
    )
    input_seg = layer_input.reshape(seg_group, seg_len, width_shard)
    up_part = jnp.einsum("sjk,srk->rsj", own_keys, up_seg, preferred_element_type=jnp.float32)
    down_part = jnp.einsum("sjd,srd->rsj", input_seg, down_seg, preferred_element_type=jnp.float32)
    lowrank, projected = lax.psum((up_part, down_part), "tensor")
    lowrank = lowrank.astype(jnp.bfloat16)
    projected = projected.astype(jnp.bfloat16)
    frozen = lax.dot_general(
        whole, key_weight, (((1,), (1,)), ((), ())), preferred_element_type=jnp.float32
    )
    extra = jnp.einsum("rsj,srd->sjd", lowrank, down_seg, preferred_element_type=jnp.float32)
    input_grad = (frozen + 2.0 * extra.reshape(tok_group, width_shard)).astype(jnp.bfloat16)
    seg_down = 2.0 * jnp.einsum(
        "rsj,sjd->srd", lowrank, input_seg, preferred_element_type=jnp.float32
    )
    seg_up = 2.0 * jnp.einsum(
        "rsj,sjk->srk", projected, own_keys, preferred_element_type=jnp.float32
    )
    seg_index = jnp.arange(seg_group, dtype=jnp.int32)
    same = seg_slot[:, None] == seg_slot[None, :]
    earlier = same & (seg_index[None, :] < seg_index[:, None])
    leading = jnp.logical_not(jnp.any(earlier, axis=1))
    merge_rows = (same & leading[:, None]).astype(jnp.float32)
    rows_down = jnp.einsum(
        "us,srd->urd", merge_rows, seg_down, precision=lax.Precision.HIGHEST
    ).astype(jnp.bfloat16)
    rows_up = jnp.einsum("us,srk->urk", merge_rows, seg_up, precision=lax.Precision.HIGHEST).astype(
        jnp.bfloat16
    )
    every_down, every_up = (
        lax.all_gather(rows_down, "dp", axis=0, tiled=True),
        lax.all_gather(rows_up, "dp", axis=0, tiled=True),
    )
    owned = group_index * per_owner + jnp.arange(per_owner, dtype=jnp.int32)
    mine = (every_slot[:, None] == owned[None, :]).astype(jnp.bfloat16)
    down_grad = jnp.einsum(
        "sp,srd->prd", mine, every_down, preferred_element_type=jnp.float32
    ).astype(jnp.bfloat16)
    up_grad = jnp.einsum("sp,srk->prk", mine, every_up, preferred_element_type=jnp.float32).astype(
        jnp.bfloat16
    )
    return (input_grad, down_grad, up_grad)


def solution(mesh):
    in_specs = (
        P("dp", "tensor"),
        P(("dp", "tensor"), None),
        P("tensor", None),
        P("dp", None, "tensor"),
        P("dp", None, "tensor"),
        P(),
        P(),
        P("dp"),
    )
    out_specs = (P("dp", "tensor"), P("dp", None, "tensor"), P("dp", None, "tensor"))
    return jax.shard_map(
        on_device, mesh=mesh, in_specs=in_specs, out_specs=out_specs, check_vma=False
    )
```

profile of v0, /device:TPU:1, one launch (start us, length us, event | category | flops | bytes accessed | tf_op | source)
XLA Modules:
  0.0 368.9 jit_solution(6331386676512770924)
XLA Ops:
  7.2 0.0 copy-start
  7.2 0.0 all-gather.6.cloned.1.call-start
  7.2 0.7 all-gather.6.cloned.1.call-update
  7.9 0.0 all-gather.4.cloned.1.call-start
  8.6 1.7 broadcast_select_fusion
  10.4 0.0 all-gather.4.cloned.1.call-update
  10.4 0.0 all-gather.8.cloned.1.call-start
  10.5 0.9 select_reduce_fusion
  11.4 0.1 dynamic_slice.6
  11.5 0.2 fusion.6
  11.7 22.9 %all_gather.16 = bf16[128,16,32]{2,1,0:T(8,128)(2,1)S(1)} all-gather(bf16[8,16,32]{2,1,0:T(8,128)(2,1)} %param.12), channel_id=1, replica_groups=mesh['dp'=16,'tensor'=32] {'dp'}, dimensions={0}, use_global_device_ids=true | all-gather | bytes 139264 | tf_op jit(solution)/shard_map/all_gather | solution.py:42
  34.5 0.4 copy.26
  35.0 0.2 convolution_convert_fusion.5
  35.1 0.2 reshape.60
  35.3 21.6 %all-gather.6.cloned.1.call-done = bf16[128,16,256]{2,1,0:T(8,128)(2,1)} async-done(((bf16[8,16,256]{2,1,0:T(8,128)(2,1)}), bf16[128,16,256]{2,1,0:T(8,128)(2,1)}) %all-gather.6.cloned.1.call-update) | async-done | bytes 1048592 | tf_op jit(solution)/shard_map/all_gather | solution.py:41
  56.9 1.6 copy.37
  58.5 0.3 convolution_convert_fusion
  58.8 0.1 copy.38
  58.9 0.0 copy-done
  58.9 1.4 convolution_bitcast_fusion
  60.3 103.2 %all-gather.4.cloned.1.call-done = bf16[4096,1024]{1,0:T(8,128)(2,1)} async-done(((bf16[128,1024]{1,0:T(8,128)(2,1)}), bf16[4096,1024]{1,0:T(8,128)(2,1)}) %all-gather.4.cloned.1.call-update) | async-done | bytes 8388624 | tf_op jit(solution)/shard_map/all_gather | solution.py:39
  163.5 1.6 constant_dynamic-slice_fusion
  165.0 1.4 convolution_bitcast_fusion.1
  166.4 117.5 %all-reduce.2 = (bf16[16,32,128]{2,0,1:T(8,128)(2,1)S(1)}, bf16[16,32,128]{2,0,1:T(8,128)(2,1)}) all-reduce(f32[16,32,128]{2,0,1:T(8,128)} %convolution_bitcast_fusion.1, f32[16,32,128]{2,0,1:T(8,128)} %convolution_bitcast_fusion), channel_id=1, replica_groups=mesh['dp'=16,'tensor'=32] {'tensor'}, use_global_device_ids=true, to_apply=%region_1.2 | all-reduce | flops 131072 | bytes 786432 | tf_op jit(solution)/shard_map/psum | solution.py:55
  283.9 0.4 convolution_multiply_fusion.1
  284.3 1.4 convolution_convert_fusion.1
  285.7 0.0 all-gather.8.cloned.1.call-update
  285.8 1.3 convolution_multiply_fusion.2
  287.0 0.4 convolution_convert_fusion.2
  287.4 0.0 copy-start.1
  287.4 57.7 %all_gather.19 = bf16[512,16,32]{2,0,1:T(8,128)(2,1)S(1)} all-gather(bf16[32,16,32]{2,0,1:T(8,128)(2,1)S(1)} %convolution_convert_fusion.2), channel_id=1, replica_groups=mesh['dp'=16,'tensor'=32] {'dp'}, dimensions={0}, use_global_device_ids=true | all-gather | bytes 557056 | tf_op jit(solution)/shard_map/all_gather | solution.py:82
  345.1 0.4 convolution_convert_fusion.4
  345.5 0.6 copy.33
  346.2 0.8 convolution_multiply_fusion
  346.9 0.0 copy-done.1
  346.9 7.5 %fusion = bf16[4096,256]{1,0:T(8,128)(2,1)} fusion(f32[4096,256]{1,0:T(8,128)S(1)} %bitcast.43, bf16[4096,1024]{1,0:T(8,128)(2,1)} %all-gather.4.cloned.1.call-done, bf16[256,1024]{1,0:T(8,128)(2,1)S(1)} %copy-done.1), kind=kOutput, calls=%fused_computation.1 | convolution fusion | flops 2149580800 | bytes 15204352 | tf_op jit(solution)/shard_map/dot_general | solution.py:58
  354.4 4.4 %all-gather.8.cloned.1.call-done = bf16[512,16,256]{2,0,1:T(8,128)(2,1)} async-done(((bf16[32,16,256]{2,0,1:T(8,128)(2,1)}), bf16[512,16,256]{2,0,1:T(8,128)(2,1)}) %all-gather.8.cloned.1.call-update) | async-done | bytes 4194320 | tf_op jit(solution)/shard_map/all_gather | solution.py:81
  358.9 2.9 convolution_convert_fusion.3
  361.7 0.7 copy.32
  (3 shorter events, 0.0 us)
Async XLA Ops:
  7.2 51.7 %copy-start = (bf16[4096,256]{1,0:T(8,128)(2,1)S(1)}, bf16[4096,256]{1,0:T(8,128)(2,1)}, u32[]{:S(2)}) copy-start(bf16[4096,256]{1,0:T(8,128)(2,1)} %param.8) | copy-start | bytes 6291460
  7.2 49.7 %all-gather.6.cloned.1.call-start = ((), (), s32[]{:S(2)}) async-start(), calls=%async_computation.1 | async-start | bytes 1114112 | tf_op jit(solution)/shard_map/all_gather | solution.py:41
  7.9 155.5 %all-gather.4.cloned.1.call-start = ((), (), s32[]{:S(2)}) async-start(), calls=%async_computation | async-start | bytes 8650752 | tf_op jit(solution)/shard_map/all_gather | solution.py:39
  10.4 348.5 %all-gather.8.cloned.1.call-start = ((), (), s32[]{:S(2)}) async-start(), calls=%async_computation.2 | async-start | bytes 4456448 | tf_op jit(solution)/shard_map/all_gather | solution.py:81
  287.4 59.5 %copy-start.1 = (bf16[256,1024]{1,0:T(8,128)(2,1)S(1)}, bf16[256,1024]{1,0:T(8,128)(2,1)}, u32[]{:S(2)}) copy-start(bf16[256,1024]{1,0:T(8,128)(2,1)} %param.10) | copy-start | bytes 1572868
Sparse Core Ops, SparseCore 0:
  10.1 46.6 all-gather.5
  60.6 102.8 all-gather.3
  285.9 72.9 all-gather.7
where the time goes:
time: 369 us
  blocking collectives  198 us (54%)
  waiting for transfers between devices  130 us (35%)
  matrix products  18.2 us (5%)
  between operations  14.5 us (4%)
  local copies, waits for them, and re-layouts  5.25 us (1%)
    psum x1, blocking collectives, on_device(): lowrank, projected = lax.psum((up_part, down_part), 'tensor')  117 us
    all_gather x1, waiting for transfers between devices, on_device(): whole = lax.all_gather(masked, 'tensor', axis=0, tiled=True)  103 us
    all_gather x1, blocking collectives, on_device(): lax.all_gather(rows_up, 'dp', axis=0, tiled=True)  57.7 us
    all_gather x1, blocking collectives, on_device(): lax.all_gather(adapter_up, 'dp', axis=0, tiled=True)  22.9 us
    all_gather x1, waiting for transfers between devices, on_device(): lax.all_gather(adapter_down, 'dp', axis=0, tiled=True)  21.6 us
    dot_general x1, matrix products, on_device(): lax.dot_general(whole, key_weight, (((1,), (1,)), ((), ())), preferred_el...  7.47 us
  transfers between devices with their start and end apart: 3, of which 3 were waited for; matrix products, arithmetic and copies ran while one was open for 5% of the time, Pallas kernels for 0%

commit v1 on v0

--- a/solution.py
+++ b/solution.py
@@ -2,6 +2,33 @@
 import jax.numpy as jnp
 from jax import lax
 from jax.sharding import PartitionSpec as P
+
+
+def detail_sample(target):
+    piece_next = lax.axis_size("dp")
+    seen_now, frame_out, val2 = (piece_next, lax.axis_index("dp"), target.shape[0])
+    shelf = tuple((s * seen_now if dev_j == 0 else s for dev_j, s in enumerate(target.shape)))
+    part_next = lax.dynamic_update_slice_in_dim(
+        jnp.zeros(shelf, target.dtype), target, frame_out * val2, axis=0
+    )
+    everything = n_now = target
+    j0 = 1
+    while j0 < seen_now // 2 + 1:
+        everything = lax.ppermute(
+            everything, "dp", tuple(((dev_j, (dev_j + 1) % seen_now) for dev_j in range(seen_now)))
+        )
+        part_next = lax.dynamic_update_slice_in_dim(
+            part_next, everything, (frame_out - j0) % seen_now * val2, axis=0
+        )
+        if 2 * j0 < seen_now:
+            n_now = lax.ppermute(
+                n_now, "dp", tuple(((dev_j, (dev_j - 1) % seen_now) for dev_j in range(seen_now)))
+            )
+            part_next = lax.dynamic_update_slice_in_dim(
+                part_next, n_now, (frame_out + j0) % seen_now * val2, axis=0
+            )
+        j0 += 1
+    return part_next
 
 
 def on_device(
@@ -79,7 +106,7 @@
     )
     every_down, every_up = (
         lax.all_gather(rows_down, "dp", axis=0, tiled=True),
-        lax.all_gather(rows_up, "dp", axis=0, tiled=True),
+        detail_sample(rows_up),
     )
     owned = group_index * per_owner + jnp.arange(per_owner, dtype=jnp.int32)
     mine = (every_slot[:, None] == owned[None, :]).astype(jnp.bfloat16)

time: 369 us -> 429 us (1.16); the launches traced: 369 us -> 422 us
  blocking collectives: 198 us -> 141 us
  local copies, waits for them, and re-layouts: 5.25 us -> 50.6 us
  starting transfers between devices: 0.12 us -> 42.9 us
  waiting for transfers between devices: 130 us -> 152 us
    all_gather x1 -> x0, blocking collectives: 57.7 us -> none  [on_device(): lax.all_gather(rows_up, 'dp', axis=0, tiled=True)]
    dynamic_update_slice x0 -> x16, local copies, waits for them, and re-layouts: none -> 44 us  [the longest x8 21.6 us: detail_sample(): lax.dynamic_update_slice_in_dim(part_next, everything, (frame_out - j0) %...]
    ppermute x0 -> x15, starting transfers between devices: none -> 42.8 us  [the longest x8 39 us: detail_sample(): lax.ppermute(everything, 'dp', tuple(((dev_j, (dev_j + 1) % seen_now) for...]
    ppermute x0 -> x15, waiting for transfers between devices: none -> 26.6 us  [the longest x7 20.2 us: detail_sample(): lax.ppermute(n_now, 'dp', tuple(((dev_j, (dev_j - 1) % seen_now) for dev_...]
    all_gather x1, waiting for transfers between devices: 4.45 us -> 0.01 us  [on_device(): lax.all_gather(rows_down, 'dp', axis=0, tiled=True)]
  transfers between devices with their start and end apart: 3 -> 18, of which waited for: 3 -> 14; matrix products, arithmetic and copies ran while one was open for 5% -> 15% of each run, Pallas kernels for 0% -> 0%
where the time goes in v1:
time: 429 us; the launch traced here: 422 us
  waiting for transfers between devices  152 us (35%)
  blocking collectives  141 us (33%)
  local copies, waits for them, and re-layouts  50.6 us (12%)
  starting transfers between devices  42.9 us (10%)
  matrix products  18.8 us (4%)
  between operations  14.7 us (3%)
    psum x1, blocking collectives, on_device(): lowrank, projected = lax.psum((up_part, down_part), 'tensor')  118 us
    all_gather x1, waiting for transfers between devices, on_device(): whole = lax.all_gather(masked, 'tensor', axis=0, tiled=True)  103 us
    ppermute x8, starting transfers between devices, detail_sample(): lax.ppermute(everything, 'dp', tuple(((dev_j, (dev_j + 1) % seen_now) for...  39 us
    all_gather x1, blocking collectives, on_device(): lax.all_gather(adapter_up, 'dp', axis=0, tiled=True)  22.9 us
    dynamic_update_slice x8, local copies, waits for them, and re-layouts, detail_sample(): lax.dynamic_update_slice_in_dim(part_next, everything, (frame_out - j0) %...  21.6 us
    all_gather x1, waiting for transfers between devices, on_device(): lax.all_gather(adapter_down, 'dp', axis=0, tiled=True)  21.6 us
    ppermute x7, waiting for transfers between devices, detail_sample(): lax.ppermute(n_now, 'dp', tuple(((dev_j, (dev_j - 1) % seen_now) for dev_...  20.2 us
    dynamic_update_slice x7, local copies, waits for them, and re-layouts, detail_sample(): lax.dynamic_update_slice_in_dim(part_next, n_now, (frame_out + j0) % seen...  19.5 us
  transfers between devices with their start and end apart: 18, of which 14 were waited for; matrix products, arithmetic and copies ran while one was open for 15% of the time, Pallas kernels for 0%

profile of v1, /device:TPU:1, one launch (start us, length us, event | category | flops | bytes accessed | tf_op | source)
XLA Modules:
  0.0 422.5 jit_solution(16863313498949463583)
XLA Ops:
  7.2 0.7 all-gather.6.cloned.1.call-update
  8.6 1.7 broadcast_select_fusion
  10.5 0.9 select_reduce_fusion
  11.5 0.2 fusion.8
  11.7 22.9 %all_gather.13 = bf16[128,16,32]{2,1,0:T(8,128)(2,1)S(1)} all-gather(bf16[8,16,32]{2,1,0:T(8,128)(2,1)} %param.12), channel_id=1, replica_groups=mesh['dp'=16,'tensor'=32] {'dp'}, dimensions={0}, use_global_device_ids=true | all-gather | bytes 139264 | tf_op jit(solution)/shard_map/all_gather | solution.py:69
  34.5 0.4 copy.26
  35.0 0.2 convolution_convert_fusion.3
  35.3 21.6 %all-gather.6.cloned.1.call-done = bf16[128,16,256]{2,1,0:T(8,128)(2,1)} async-done(((bf16[8,16,256]{2,1,0:T(8,128)(2,1)}), bf16[128,16,256]{2,1,0:T(8,128)(2,1)}) %all-gather.6.cloned.1.call-update) | async-done | bytes 1048592 | tf_op jit(solution)/shard_map/all_gather | solution.py:68
  56.9 1.6 copy.37
  58.5 0.3 convolution_convert_fusion
  58.9 1.4 convolution_bitcast_fusion
  60.3 103.2 %all-gather.4.cloned.1.call-done = bf16[4096,1024]{1,0:T(8,128)(2,1)} async-done(((bf16[128,1024]{1,0:T(8,128)(2,1)}), bf16[4096,1024]{1,0:T(8,128)(2,1)}) %all-gather.4.cloned.1.call-update) | async-done | bytes 8388624 | tf_op jit(solution)/shard_map/all_gather | solution.py:66
  163.5 1.6 constant_dynamic-slice_fusion
  165.0 1.4 convolution_bitcast_fusion.1
  166.4 117.7 %all-reduce.2 = (bf16[16,32,128]{2,0,1:T(8,128)(2,1)S(1)}, bf16[16,32,128]{2,0,1:T(8,128)(2,1)}) all-reduce(f32[16,32,128]{2,0,1:T(8,128)} %convolution_bitcast_fusion.1, f32[16,32,128]{2,0,1:T(8,128)} %convolution_bitcast_fusion), channel_id=1, replica_groups=mesh['dp'=16,'tensor'=32] {'tensor'}, use_global_device_ids=true, to_apply=%region_1.2 | all-reduce | flops 131072 | bytes 786432 | tf_op jit(solution)/shard_map/psum | solution.py:82
  284.1 0.4 convolution_multiply_fusion.1
  284.5 1.4 convolution_convert_fusion.1
  285.9 2.0 convolution_multiply_fusion.2
  287.9 1.1 copy.31
  289.0 0.3 fusion.5
  289.4 29.5 %collective-permute-start = (bf16[32,16,32]{0,2,1:T(8,128)(2,1)S(1)}, bf16[32,16,32]{0,2,1:T(8,128)(2,1)S(1)}, u32[]{:S(2)}, u32[]{:S(2)}) collective-permute-start(bf16[32,16,32]{0,2,1:T(8,128)(2,1)S(1)} %convert_element_type.37), channel_id=1, source_target_pairs={{0,32},{32,64},{64,96},{96,128},{128,160},{160,192},{192,224},{224... | collective-permute-start | bytes 98312 | tf_op jit(solution)/shard_map/ppermute | solution.py:17
  318.9 1.9 collective-permute-done
  320.9 2.4 collective-permute-start.2
  323.4 2.4 collective-permute-done.2
  325.9 2.5 collective-permute-start.4
  328.4 2.1 collective-permute-done.3
  330.5 0.5 collective-permute-done.4
  331.1 1.8 collective-permute-start.6
  333.0 4.7 %collective-permute-done.5 = bf16[32,16,32]{0,2,1:T(8,128)(2,1)S(1)} collective-permute-done((bf16[32,16,32]{0,2,1:T(8,128)(2,1)S(1)}, bf16[32,16,32]{0,2,1:T(8,128)(2,1)S(1)}, u32[]{:S(2)}, u32[]{:S(2)}) %collective-permute-start.5) | collective-permute-done | bytes 32800 | tf_op jit(solution)/shard_map/ppermute | solution.py:24
  337.7 0.4 collective-permute-start.7
  338.2 1.5 collective-permute-start.8
  339.7 5.2 %collective-permute-done.7 = bf16[32,16,32]{0,2,1:T(8,128)(2,1)S(1)} collective-permute-done((bf16[32,16,32]{0,2,1:T(8,128)(2,1)S(1)}, bf16[32,16,32]{0,2,1:T(8,128)(2,1)S(1)}, u32[]{:S(2)}, u32[]{:S(2)}) %collective-permute-start.7) | collective-permute-done | bytes 32800 | tf_op jit(solution)/shard_map/ppermute | solution.py:24
  344.9 0.6 collective-permute-start.9
  345.5 0.4 collective-permute-done.8
  345.8 0.8 collective-permute-start.10
  346.6 5.8 %collective-permute-done.9 = bf16[32,16,32]{0,2,1:T(8,128)(2,1)} collective-permute-done((bf16[32,16,32]{0,2,1:T(8,128)(2,1)S(1)}, bf16[32,16,32]{0,2,1:T(8,128)(2,1)}, u32[]{:S(2)}, u32[]{:S(2)}) %collective-permute-start.9) | collective-permute-done | bytes 32800 | tf_op jit(solution)/shard_map/ppermute | solution.py:24
  352.4 0.7 collective-permute-start.11
  353.1 0.6 collective-permute-done.10
  353.7 0.4 collective-permute-start.12
  354.2 0.7 convolution_multiply_fusion
  354.9 2.5 collective-permute-done.11
  357.4 1.9 collective-permute-start.13
  359.3 0.4 collective-permute-done.12
  359.7 7.3 %fusion = bf16[4096,256]{1,0:T(8,128)(2,1)} fusion(f32[4096,256]{1,0:T(8,128)S(1)} %bitcast.45, bf16[4096,1024]{1,0:T(8,128)(2,1)} %all-gather.4.cloned.1.call-done, bf16[256,1024]{1,0:T(8,128)(2,1)S(1)} %copy-done.9), kind=kOutput, calls=%fused_computation.1 | convolution fusion | flops 2149580800 | bytes 15204352 | tf_op jit(solution)/shard_map/dot_general | solution.py:85
  367.1 2.9 dynamic_update_slice.48
  370.0 0.6 dynamic_update_slice.49
  370.6 2.9 dynamic_update_slice.50
  373.5 2.8 dynamic_update_slice.51
  376.4 2.9 dynamic_update_slice.52
  379.3 2.8 dynamic_update_slice.53
  382.1 1.4 dynamic_update_slice.54
  383.5 3.6 dynamic_update_slice.55
  387.1 3.7 dynamic_update_slice.56
  390.8 1.5 dynamic_update_slice.57
  392.3 3.7 dynamic_update_slice.58
  396.0 3.7 dynamic_update_slice.59
  399.7 3.7 dynamic_update_slice.60
  403.3 3.7 dynamic_update_slice.61
  407.0 1.4 dynamic_update_slice.62
  408.4 2.9 dynamic_update_slice.63
  411.3 0.5 convolution_convert_fusion.4
  411.8 0.6 copy.33
  412.4 2.9 convolution_convert_fusion.2
  415.3 0.7 copy.32
  (42 shorter events, 1.0 us)
Async XLA Ops:
  7.2 51.7 %copy-start = (bf16[4096,256]{1,0:T(8,128)(2,1)S(1)}, bf16[4096,256]{1,0:T(8,128)(2,1)}, u32[]{:S(2)}) copy-start(bf16[4096,256]{1,0:T(8,128)(2,1)} %param.8) | copy-start | bytes 6291460
  7.2 49.7 %all-gather.6.cloned.1.call-start = ((), (), s32[]{:S(2)}) async-start(), calls=%async_computation.1 | async-start | bytes 1114112 | tf_op jit(solution)/shard_map/all_gather | solution.py:68
  7.9 155.5 %all-gather.4.cloned.1.call-start = ((), (), s32[]{:S(2)}) async-start(), calls=%async_computation | async-start | bytes 8650752 | tf_op jit(solution)/shard_map/all_gather | solution.py:66
  10.4 402.0 %all-gather.8.cloned.1.call-start = ((), (), s32[]{:S(2)}) async-start(), calls=%async_computation.2 | async-start | bytes 4456448 | tf_op jit(solution)/shard_map/all_gather | solution.py:108
  289.4 31.5 %collective-permute-start = (bf16[32,16,32]{0,2,1:T(8,128)(2,1)S(1)}, bf16[32,16,32]{0,2,1:T(8,128)(2,1)S(1)}, u32[]{:S(2)}, u32[]{:S(2)}) collective-permute-start(bf16[32,16,32]{0,2,1:T(8,128)(2,1)S(1)} %convert_element_type.37), channel_id=1, source_target_pairs={{0,32},{32,64},{64,96},{96,128},{128,160},{160,192},{192,224},{224... | collective-permute-start | bytes 98312 | tf_op jit(solution)/shard_map/ppermute | solution.py:17
  318.9 4.4 %collective-permute-start.1 = (bf16[32,16,32]{0,2,1:T(8,128)(2,1)S(1)}, bf16[32,16,32]{0,2,1:T(8,128)(2,1)S(1)}, u32[]{:S(2)}, u32[]{:S(2)}) collective-permute-start(bf16[32,16,32]{0,2,1:T(8,128)(2,1)S(1)} %convert_element_type.37), channel_id=1, source_target_pairs={{0,480},{32,0},{64,32},{96,64},{128,96},{160,128},{192,160},{224,1... | collective-permute-start | bytes 98312 | tf_op jit(solution)/shard_map/ppermute | solution.py:24
  320.9 5.0 %collective-permute-start.2 = (bf16[32,16,32]{0,2,1:T(8,128)(2,1)S(1)}, bf16[32,16,32]{0,2,1:T(8,128)(2,1)S(1)}, u32[]{:S(2)}, u32[]{:S(2)}) collective-permute-start(bf16[32,16,32]{0,2,1:T(8,128)(2,1)S(1)} %collective-permute-done), channel_id=1, source_target_pairs={{0,32},{32,64},{64,96},{96,128},{128,160},{160,192},{192,224},{224... | collective-permute-start | bytes 98312 | tf_op jit(solution)/shard_map/ppermute | solution.py:17
  323.3 7.2 %collective-permute-start.3 = (bf16[32,16,32]{0,2,1:T(8,128)(2,1)S(1)}, bf16[32,16,32]{0,2,1:T(8,128)(2,1)S(1)}, u32[]{:S(2)}, u32[]{:S(2)}) collective-permute-start(bf16[32,16,32]{0,2,1:T(8,128)(2,1)S(1)} %collective-permute-done.1), channel_id=1, source_target_pairs={{0,480},{32,0},{64,32},{96,64},{128,96},{160,128},{192,160},{224,1... | collective-permute-start | bytes 98312 | tf_op jit(solution)/shard_map/ppermute | solution.py:24
  325.9 5.1 %collective-permute-start.4 = (bf16[32,16,32]{0,2,1:T(8,128)(2,1)S(1)}, bf16[32,16,32]{0,2,1:T(8,128)(2,1)S(1)}, u32[]{:S(2)}, u32[]{:S(2)}) collective-permute-start(bf16[32,16,32]{0,2,1:T(8,128)(2,1)S(1)} %collective-permute-done.2), channel_id=1, source_target_pairs={{0,32},{32,64},{64,96},{96,128},{128,160},{160,192},{192,224},{224... | collective-permute-start | bytes 98312 | tf_op jit(solution)/shard_map/ppermute | solution.py:17
  330.5 0.7 copy-start.1
  330.5 7.2 %collective-permute-start.5 = (bf16[32,16,32]{0,2,1:T(8,128)(2,1)S(1)}, bf16[32,16,32]{0,2,1:T(8,128)(2,1)S(1)}, u32[]{:S(2)}, u32[]{:S(2)}) collective-permute-start(bf16[32,16,32]{0,2,1:T(8,128)(2,1)S(1)} %collective-permute-done.3), channel_id=1, source_target_pairs={{0,480},{32,0},{64,32},{96,64},{128,96},{160,128},{192,160},{224,1... | collective-permute-start | bytes 98312 | tf_op jit(solution)/shard_map/ppermute | solution.py:24
  331.1 6.5 %copy-start.3 = (bf16[32,16,32]{0,2,1:T(8,128)(2,1)}, bf16[32,16,32]{0,2,1:T(8,128)(2,1)S(1)}, u32[]{:S(2)}) copy-start(bf16[32,16,32]{0,2,1:T(8,128)(2,1)S(1)} %collective-permute-done.4) | copy-start | bytes 98308
  331.1 7.1 %collective-permute-start.6 = (bf16[32,16,32]{0,2,1:T(8,128)(2,1)S(1)}, bf16[32,16,32]{0,2,1:T(8,128)(2,1)S(1)}, u32[]{:S(2)}, u32[]{:S(2)}) collective-permute-start(bf16[32,16,32]{0,2,1:T(8,128)(2,1)S(1)} %collective-permute-done.4), channel_id=1, source_target_pairs={{0,32},{32,64},{64,96},{96,128},{128,160},{160,192},{192,224},{224... | collective-permute-start | bytes 98312 | tf_op jit(solution)/shard_map/ppermute | solution.py:17
  337.6 22.0 %copy-start.5 = (bf16[32,16,32]{0,2,1:T(8,128)(2,1)}, bf16[32,16,32]{0,2,1:T(8,128)(2,1)S(1)}, u32[]{:S(2)}) copy-start(bf16[32,16,32]{0,2,1:T(8,128)(2,1)S(1)} %collective-permute-done.5) | copy-start | bytes 98308
  337.7 7.2 %collective-permute-start.7 = (bf16[32,16,32]{0,2,1:T(8,128)(2,1)S(1)}, bf16[32,16,32]{0,2,1:T(8,128)(2,1)S(1)}, u32[]{:S(2)}, u32[]{:S(2)}) collective-permute-start(bf16[32,16,32]{0,2,1:T(8,128)(2,1)S(1)} %collective-permute-done.5), channel_id=1, source_target_pairs={{0,480},{32,0},{64,32},{96,64},{128,96},{160,128},{192,160},{224,1... | collective-permute-start | bytes 98312 | tf_op jit(solution)/shard_map/ppermute | solution.py:24
  338.2 21.5 %copy-start.6 = (bf16[32,16,32]{0,2,1:T(8,128)(2,1)}, bf16[32,16,32]{0,2,1:T(8,128)(2,1)S(1)}, u32[]{:S(2)}) copy-start(bf16[32,16,32]{0,2,1:T(8,128)(2,1)S(1)} %collective-permute-done.6) | copy-start | bytes 98308
  338.2 7.6 %collective-permute-start.8 = (bf16[32,16,32]{0,2,1:T(8,128)(2,1)S(1)}, bf16[32,16,32]{0,2,1:T(8,128)(2,1)S(1)}, u32[]{:S(2)}, u32[]{:S(2)}) collective-permute-start(bf16[32,16,32]{0,2,1:T(8,128)(2,1)S(1)} %collective-permute-done.6), channel_id=1, source_target_pairs={{0,32},{32,64},{64,96},{96,128},{128,160},{160,192},{192,224},{224... | collective-permute-start | bytes 98312 | tf_op jit(solution)/shard_map/ppermute | solution.py:17
  344.9 14.8 %copy-start.7 = (bf16[32,16,32]{0,2,1:T(8,128)(2,1)}, bf16[32,16,32]{0,2,1:T(8,128)(2,1)S(1)}, u32[]{:S(2)}) copy-start(bf16[32,16,32]{0,2,1:T(8,128)(2,1)S(1)} %collective-permute-done.7) | copy-start | bytes 98308
  344.9 7.5 %collective-permute-start.9 = (bf16[32,16,32]{0,2,1:T(8,128)(2,1)S(1)}, bf16[32,16,32]{0,2,1:T(8,128)(2,1)}, u32[]{:S(2)}, u32[]{:S(2)}) collective-permute-start(bf16[32,16,32]{0,2,1:T(8,128)(2,1)S(1)} %collective-permute-done.7), channel_id=1, source_target_pairs={{0,480},{32,0},{64,32},{96,64},{128,96},{160,128},{192,160},{224,1... | collective-permute-start | bytes 98312 | tf_op jit(solution)/shard_map/ppermute | solution.py:24
  345.8 13.9 %copy-start.8 = (bf16[32,16,32]{0,2,1:T(8,128)(2,1)}, bf16[32,16,32]{0,2,1:T(8,128)(2,1)S(1)}, u32[]{:S(2)}) copy-start(bf16[32,16,32]{0,2,1:T(8,128)(2,1)S(1)} %collective-permute-done.8) | copy-start | bytes 98308
  345.8 7.9 %collective-permute-start.10 = (bf16[32,16,32]{0,2,1:T(8,128)(2,1)S(1)}, bf16[32,16,32]{0,2,1:T(8,128)(2,1)}, u32[]{:S(2)}, u32[]{:S(2)}) collective-permute-start(bf16[32,16,32]{0,2,1:T(8,128)(2,1)S(1)} %collective-permute-done.8), channel_id=1, source_target_pairs={{0,32},{32,64},{64,96},{96,128},{128,160},{160,192},{192,224},{224... | collective-permute-start | bytes 98312 | tf_op jit(solution)/shard_map/ppermute | solution.py:17
  346.6 13.1 %copy-start.9 = (bf16[256,1024]{1,0:T(8,128)(2,1)S(1)}, bf16[256,1024]{1,0:T(8,128)(2,1)}, u32[]{:S(2)}) copy-start(bf16[256,1024]{1,0:T(8,128)(2,1)} %param.10) | copy-start | bytes 1572868
  352.4 5.0 %collective-permute-start.11 = (bf16[32,16,32]{0,2,1:T(8,128)(2,1)}, bf16[32,16,32]{0,2,1:T(8,128)(2,1)}, u32[]{:S(2)}, u32[]{:S(2)}) collective-permute-start(bf16[32,16,32]{0,2,1:T(8,128)(2,1)} %collective-permute-done.9), channel_id=1, source_target_pairs={{0,480},{32,0},{64,32},{96,64},{128,96},{160,128},{192,160},{224,1... | collective-permute-start | bytes 98312 | tf_op jit(solution)/shard_map/ppermute | solution.py:24
  353.7 5.9 %collective-permute-start.12 = (bf16[32,16,32]{0,2,1:T(8,128)(2,1)}, bf16[32,16,32]{0,2,1:T(8,128)(2,1)}, u32[]{:S(2)}, u32[]{:S(2)}) collective-permute-start(bf16[32,16,32]{0,2,1:T(8,128)(2,1)} %collective-permute-done.10), channel_id=1, source_target_pairs={{0,32},{32,64},{64,96},{96,128},{128,160},{160,192},{192,224},{224... | collective-permute-start | bytes 98312 | tf_op jit(solution)/shard_map/ppermute | solution.py:17
  357.4 49.6 %collective-permute-start.13 = (bf16[32,16,32]{0,2,1:T(8,128)(2,1)}, bf16[32,16,32]{0,2,1:T(8,128)(2,1)}, u32[]{:S(2)}, u32[]{:S(2)}) collective-permute-start(bf16[32,16,32]{0,2,1:T(8,128)(2,1)} %collective-permute-done.11), channel_id=1, source_target_pairs={{0,480},{32,0},{64,32},{96,64},{128,96},{160,128},{192,160},{224,1... | collective-permute-start | bytes 98312 | tf_op jit(solution)/shard_map/ppermute | solution.py:24
  359.7 48.7 %collective-permute-start.14 = (bf16[32,16,32]{0,2,1:T(8,128)(2,1)}, bf16[32,16,32]{0,2,1:T(8,128)(2,1)S(1)}, u32[]{:S(2)}, u32[]{:S(2)}) collective-permute-start(bf16[32,16,32]{0,2,1:T(8,128)(2,1)} %collective-permute-done.12), channel_id=1, source_target_pairs={{0,32},{32,64},{64,96},{96,128},{128,160},{160,192},{192,224},{224... | collective-permute-start | bytes 98312 | tf_op jit(solution)/shard_map/ppermute | solution.py:17
  359.7 16.7 %copy-start.2 = (bf16[32,16,32]{0,2,1:T(8,128)(2,1)S(1)}, bf16[32,16,32]{0,2,1:T(8,128)(2,1)}, u32[]{:S(2)}) copy-start(bf16[32,16,32]{0,2,1:T(8,128)(2,1)} %copy-done.1) | copy-start | bytes 98308
  359.7 19.6 %copy-start.4 = (bf16[32,16,32]{0,2,1:T(8,128)(2,1)S(1)}, bf16[32,16,32]{0,2,1:T(8,128)(2,1)}, u32[]{:S(2)}) copy-start(bf16[32,16,32]{0,2,1:T(8,128)(2,1)} %copy-done.3) | copy-start | bytes 98308
Sparse Core Ops, SparseCore 0:
  10.1 46.6 all-gather.5
  60.6 102.8 all-gather.3
  286.0 71.5 all-gather.7
